TPU v7x, 256 devices: a whole 4x4x8 slice. The times are simulated.
256 devices in a mesh: row: 8 (over z), col: 32 (over y, x, core).
Axes of the slice: x: 4, y: 4, z: 8, core: 2. Of those that a mesh axis runs over, the one named last changes fastest.
Arguments:
- embeds: bfloat16 [24576, 768], P('col'), may hold values from -6 to 6
- labels: bfloat16 [24576, 1000], P('col'), may hold values from -6 to 6
- sharpness: float32 [24576], P('col'), may hold values from 0.5 to 100
- pattern: int32 [192, 16], P('col'), may hold values from 0 to 191, as said below
- mask_pos: int32 [24576, 50], P('col'), may hold values from 0 to 2047, as said below
Outputs:
- propagated: bfloat16 [24576, 1000], P('col', 'row')
Inputs may be any that keep to these rules, and one draw needn't show every extreme that they name: `pattern`: split the row blocks into runs of 6 and the slots into runs of 2; within one run of row blocks and one run of slots, ids that lie in the same run of 6 block ids are equal. `mask_pos`: the 50 positions of a row are distinct; position k * 128 + m names row m of the row block's k-th candidate block.
All inputs are finite; a program needn't handle non-finite values.
Results may differ from a plain program's by a relative error of at most 0.012.
Values may be sent and summed in bfloat16 or wider, within the bound.
No kernel may reach another device: no remote copies, remote signals or barrier semaphores. Data moves between devices by JAX's collectives and lax.ppermute only.
A program may use at most 128 MiB of HBM per device.

v0:
```python
import math

import jax
import jax.numpy as jnp
from jax import lax
from jax.sharding import PartitionSpec as P

BLOCK = 128
SLOTS = 16


mixing = 0.75
lowest_logit = -1e30


COL = ("chip", "core")


def gather_columns(x):
    rows_here, width = x.shape
    same_core = lax.all_gather(x, "chip", tiled=True).reshape(-1, BLOCK, width)
    other_core = lax.ppermute(same_core, "core", [(0, 1), (1, 0)])
    return same_core, other_core


def body(embeds, labels, sharpness, pattern, mask_pos):
    rows_here, width = embeds.shape
    classes = labels.shape[1]
    n_col = lax.axis_size(COL)
    n_row = lax.axis_size("row")
    row_pos = lax.axis_index("row")
    blocks_here = rows_here // BLOCK
    slots_here = SLOTS // n_row
    span = slots_here * BLOCK
    per_device = classes // n_row
    owners = pattern // blocks_here
    local_ids = pattern % blocks_here
    my_owners = lax.dynamic_slice_in_dim(owners, row_pos * slots_here, slots_here, 1)
    my_ids = lax.dynamic_slice_in_dim(local_ids, row_pos * slots_here, slots_here, 1)
    peers = jnp.arange(n_col, dtype=jnp.int32)
    wanted = jnp.max(jnp.where(my_owners[..., None] == peers, my_ids[..., None], 0), axis=(0, 1))
    requested = lax.all_to_all(wanted, COL, split_axis=0, concat_axis=0, tiled=True)
    embedding_tiles = embeds.reshape(blocks_here, BLOCK, width)
    send_emb = embedding_tiles[requested]
    my_labels = lax.dynamic_slice_in_dim(labels, row_pos * per_device, per_device, 1)
    lanes = -(-per_device // 128) * 128
    my_labels = jnp.pad(my_labels, ((0, 0), (0, lanes - per_device)))
    all_labels = gather_columns(my_labels)
    shifted = mask_pos - row_pos * span
    shifted = jnp.where((shifted >= 0) & (shifted < span), shifted, span)
    positions = jnp.arange(span, dtype=jnp.int32)
    in_mask = jnp.any(shifted[:, :, None] == positions[None, None, :], axis=1)
    in_mask = in_mask.reshape(blocks_here, BLOCK, span)

    fetched_emb = lax.all_to_all(send_emb, COL, split_axis=0, concat_axis=0, tiled=True)
    candidate_ids = fetched_emb[my_owners].reshape(blocks_here, span, width)
    scores = jnp.einsum(
        "evg,erg->evr", embedding_tiles, candidate_ids, preferred_element_type=jnp.float32
    ) / math.sqrt(width)
    logits = scores * sharpness.reshape(blocks_here, BLOCK, 1)
    local_max = jnp.max(jnp.where(in_mask, logits, lowest_logit), axis=2)
    local_sum = jnp.sum(jnp.where(in_mask, jnp.exp(logits - local_max[..., None]), 0.0), axis=2)
    local_weights = jnp.where(
        in_mask, jnp.exp(logits - local_max[..., None]), 0.0
    ).astype(jnp.bfloat16)
    stats = lax.all_gather(jnp.stack([local_max, local_sum]), "row")
    all_weights = lax.all_gather(local_weights, "row")
    top = jnp.max(stats[:, 0], axis=0)
    totals = jnp.sum(stats[:, 1] * jnp.exp(stats[:, 0] - top), axis=0)
    factors = jnp.exp(stats[:, 0] - top) / totals

    shard_of = pattern // blocks_here
    on_this_core = (shard_of % 2 == lax.axis_index("core"))[..., None, None]
    pair_ids = (shard_of // 2) * blocks_here + pattern % blocks_here

    def propagate_using(gathered, seed, whole=False):
        gathered_lanes = seed.shape[-1]
        if whole:
            candidates = gathered[pattern]
        else:
            same_core, other_core = gathered
            candidates = jnp.where(on_this_core, same_core[pair_ids], other_core[pair_ids])
        candidates = candidates.reshape(blocks_here, n_row, span, gathered_lanes)
        pieces = jnp.einsum(
            "gtmk,tgkc->gtmc", all_weights, candidates, preferred_element_type=jnp.float32
        )
        pieces = (pieces * factors[..., None]).astype(jnp.bfloat16)
        summed = jnp.sum(pieces.astype(jnp.float32), axis=0).reshape(rows_here, gathered_lanes)
        return (mixing * summed + (1.0 - mixing) * seed.astype(jnp.float32)).astype(jnp.bfloat16)

    spread = propagate_using(all_labels, my_labels)
    whole_spread = lax.all_gather(spread[:, :per_device], COL, tiled=True)
    whole_spread = whole_spread.reshape(-1, BLOCK, per_device)
    return propagate_using(whole_spread, my_labels[:, :per_device], whole=True)


def solution(mesh):
    devices = mesh.devices
    fine = jax.sharding.Mesh(
        devices.reshape(devices.shape[0], devices.shape[1] // 2, 2), ("row", "chip", "core")
    )
    placed = (P(COL, None), P(COL, None), P(COL), P(COL, None), P(COL, None))
    return jax.shard_map(
        body, mesh=fine, in_specs=placed, out_specs=P(COL, "row"), check_vma=False
    )
```

profile of v0, /device:TPU:1, one launch (start us, length us, event | category | flops | bytes accessed | tf_op | source)
XLA Modules:
  0.0 252.2 jit_solution(3440076853180822311)
XLA Ops:
  6.5 0.0 copy-start
  6.5 0.8 fusion.23
  7.4 0.7 compare_select_fusion.1
  8.1 0.1 compare_select_fusion.3
  8.1 0.1 fusion.22
  8.2 0.1 copy.42
  8.3 15.3 %all_to_all.17 = s32[32,1,1]{2,1,0:T(1,128)S(1)} all-to-all(s32[32,1,1]{2,1,0:T(1,128)S(1)} %copy.42), channel_id=1, replica_groups=mesh['row'=8,'chip'=16,'core'=2] {'chip','core'}, dimensions={0} | all-to-all | bytes 256 | tf_op jit(solution)/shard_map/all_to_all | solution.py:42
  23.7 0.7 reduce.1
  24.4 4.9 %gather_fusion = bf16[32,128,768]{2,1,0:T(8,128)(2,1)} fusion(bf16[6,128,768]{2,1,0:T(8,128)(2,1)} %bitcast.49, s32[1024]{0:T(1024)S(1)} %pad_clamp_fusion.3), kind=kCustom, calls=%fused_computation | custom fusion | bytes 12583040 | tf_op jit(solution)/shard_map/gather | solution.py:44
  29.2 0.0 copy-start.2
  29.2 0.0 copy-start.3
  29.2 5.3 %all-to-all-start.1 = ((bf16[32,128,768]{2,1,0:T(8,128)(2,1)}), bf16[32,128,768]{2,1,0:T(8,128)(2,1)}, u32[]{:S(2)}, u32[]{:S(2)}) async-start(bf16[32,128,768]{2,1,0:T(8,128)(2,1)} %gather_fusion), calls=%async_computation.1 | async-start | bytes 12582912 | tf_op jit(solution)/shard_map/all_to_all | solution.py:55
  34.5 0.0 all-gather.6.cloned.1.call-start
  34.6 0.0 copy-done
  34.6 0.1 constant_dynamic-slice_fusion
  34.6 0.2 copy.51
  34.8 0.0 copy-start.1
  34.8 0.7 pad.4
  35.5 0.0 all-gather.6.cloned.1.call-update
  35.6 0.0 all-gather.10.cloned.1.call-start
  35.6 0.1 reshape.92
  35.7 0.0 copy-done.2
  35.7 7.2 %fusion = pred[768,256]{1,0:T(8,128)(4,1)S(1)} fusion(s32[768,50]{0,1:T(8,128)S(1)} %and_select_fusion), kind=kLoop, calls=%fused_computation.6 | loop fusion | flops 19464192 | bytes 350208 | tf_op jit(solution)/shard_map/reduce_or | solution.py:52
  43.0 0.3 copy.44
  43.3 0.0 copy-done.3
  43.3 68.2 %all-to-all-done.1 = bf16[32,128,768]{2,1,0:T(8,128)(2,1)} async-done(((bf16[32,128,768]{2,1,0:T(8,128)(2,1)}), bf16[32,128,768]{2,1,0:T(8,128)(2,1)}, u32[]{:S(2)}, u32[]{:S(2)}) %all-to-all-start.1) | async-done | bytes 6291488 | tf_op jit(solution)/shard_map/all_to_all | solution.py:55
  111.5 5.2 %gather_fusion.1 = bf16[12,128,768]{2,1,0:T(8,128)(2,1)} fusion(bf16[32,128,768]{2,1,0:T(8,128)(2,1)} %all-to-all-done.1, s32[1024]{0:T(1024)S(1)} %pad_clamp_fusion.2), kind=kCustom, calls=%fused_computation.1 | custom fusion | bytes 4718640 | tf_op jit(solution)/shard_map/gather | solution.py:56
  116.8 0.0 copy-done.1
  116.8 2.5 select_reduce_fusion
  119.3 0.2 fusion.15
  119.5 1.0 copy.45
  120.4 0.0 all-gather.10.cloned.1.call-update
  120.5 0.0 all-gather.8.cloned.1.call-start
  120.5 8.6 %all-gather.6.cloned.1.call-done = bf16[12288,128]{1,0:T(8,128)(2,1)} async-done(((bf16[768,128]{1,0:T(8,128)(2,1)}), bf16[12288,128]{1,0:T(8,128)(2,1)}) %all-gather.6.cloned.1.call-update) | async-done | bytes 3145744 | tf_op jit(solution)/shard_map/all_gather | solution.py:21
  129.1 1.3 collective-permute-start
  130.4 0.1 reshape.100
  130.5 0.1 broadcast_in_dim.63
  130.6 4.6 %gather_fusion.2 = bf16[96,128,128]{2,1,0:T(8,128)(2,1)} fusion(bf16[96,128,128]{2,1,0:T(8,128)(2,1)} %bitcast.52, s32[1024]{0:T(1024)S(1)} %pad_clamp_fusion.1), kind=kCustom, calls=%fused_computation.2 | custom fusion | bytes 6291840 | tf_op jit(solution)/shard_map/gather | solution.py:82
  135.2 22.3 %all-gather.1 = f32[16,6,128]{2,1,0:T(8,128)S(1)} all-gather(f32[2,6,128]{2,1,0:T(8,128)S(1)} %pad_maximum_fusion), channel_id=3, replica_groups=mesh['row'=8,'chip'=16,'core'=2] {'row'}, dimensions={0}, use_global_device_ids=true | all-gather | bytes 55296 | tf_op jit(solution)/shard_map/all_gather | solution.py:66
  157.6 0.0 collective-permute-done
  157.6 4.7 %gather_fusion.3 = bf16[96,128,128]{2,1,0:T(8,128)(2,1)} fusion(bf16[96,128,128]{2,1,0:T(8,128)(2,1)} %collective-permute-done, s32[1024]{0:T(1024)S(1)} %pad_clamp_fusion.1), kind=kCustom, calls=%fused_computation.3 | custom fusion | bytes 6291840 | tf_op jit(solution)/shard_map/gather | solution.py:82
  162.3 13.1 %all-gather.10.cloned.1.call-done = bf16[48,128,256]{2,1,0:T(8,128)(2,1)} async-done(((bf16[6,128,256]{2,1,0:T(8,128)(2,1)}), bf16[48,128,256]{2,1,0:T(8,128)(2,1)}) %all-gather.10.cloned.1.call-update) | async-done | bytes 3145744 | tf_op jit(solution)/shard_map/all_gather | solution.py:67
  175.4 5.9 %convert_reduce_fusion.1 = f32[6,128,128]{2,1,0:T(8,128)S(1)} fusion(f32[8,6,128]{2,1,0:T(8,128)S(1)} %fusion.21, bf16[8,6,128,256]{3,2,1,0:T(8,128)(2,1)} %bitcast.66, bf16[6,8,256,128]{3,2,1,0:T(8,128)(2,1)} %bitcast.53, bf16[6,8,256,128]{3,2,1,0:T(8,128)(2,1)} %bitcast.54, pred[6,8,256]{2,1,0:T(8,128)(4,1)S(1)} %broadcast_in_dim.64), kind=kOutput, calls=%fused_computation.13 | convolution fusion | flops 407273472 | bytes 9867264 | tf_op jit(solution)/shard_map/gtmk,tgkc->gtmc/dot_general | solution.py:84
  181.3 0.7 fusion.16
  182.0 0.0 all-gather.8.cloned.1.call-update
  182.1 0.1 reshape.116
  182.1 53.4 %all-gather.8.cloned.1.call-done = bf16[24576,125]{1,0:T(8,128)(2,1)} async-done(((bf16[768,125]{1,0:T(8,128)(2,1)}), bf16[24576,125]{1,0:T(8,128)(2,1)}) %all-gather.8.cloned.1.call-update) | async-done | bytes 6144016 | tf_op jit(solution)/shard_map/all_gather | solution.py:92
  235.5 5.5 %gather_fusion.4 = bf16[96,128,125]{2,1,0:T(8,128)(2,1)} fusion(bf16[192,128,125]{2,1,0:T(8,128)(2,1)} %bitcast.58, s32[1024]{0:T(1024)S(1)} %pad_clamp_fusion), kind=kCustom, calls=%fused_computation.4 | custom fusion | bytes 6144384 | tf_op jit(solution)/shard_map/gather | solution.py:79
  241.0 3.9 %convert_reduce_fusion = f32[6,128,125]{2,1,0:T(8,128)S(1)} fusion(f32[8,6,128]{2,1,0:T(8,128)S(1)} %fusion.21, bf16[8,6,128,256]{3,2,1,0:T(8,128)(2,1)} %bitcast.67, bf16[6,8,256,125]{3,2,1,0:T(8,128)(2,1)} %bitcast.55), kind=kOutput, calls=%fused_computation.11 | convolution fusion | flops 396192000 | bytes 6626304 | tf_op jit(solution)/shard_map/gtmk,tgkc->gtmc/dot_general | solution.py:84
  244.9 0.7 fusion.17
  (14 shorter events, 0.2 us)
Async XLA Ops:
  6.5 28.0 %copy-start = (bf16[768,1000]{0,1:T(8,128)(2,1)S(1)}, bf16[768,1000]{0,1:T(8,128)(2,1)}, u32[]{:S(2)}) copy-start(bf16[768,1000]{0,1:T(8,128)(2,1)} %param.6) | copy-start | bytes 4608004
  29.2 6.5 %copy-start.2 = (s32[768,50]{0,1:T(8,128)S(1)}, s32[768,50]{0,1:T(8,128)}, u32[]{:S(2)}) copy-start(s32[768,50]{0,1:T(8,128)} %param.9) | copy-start | bytes 460804
  29.2 14.0 %copy-start.3 = (f32[768]{0:T(1024)S(1)}, f32[768]{0:T(1024)}, u32[]{:S(2)}) copy-start(f32[768]{0:T(1024)} %param.7) | copy-start | bytes 9220
  29.2 82.3 %all-to-all-start.1 = ((bf16[32,128,768]{2,1,0:T(8,128)(2,1)}), bf16[32,128,768]{2,1,0:T(8,128)(2,1)}, u32[]{:S(2)}, u32[]{:S(2)}) async-start(bf16[32,128,768]{2,1,0:T(8,128)(2,1)} %gather_fusion), calls=%async_computation.1 | async-start | bytes 12582912 | tf_op jit(solution)/shard_map/all_to_all | solution.py:55
  34.5 94.6 %all-gather.6.cloned.1.call-start = ((), (), s32[]{:S(2)}) async-start(), calls=%async_computation.2 | async-start | bytes 3342336 | tf_op jit(solution)/shard_map/all_gather | solution.py:21
  34.8 82.0 %copy-start.1 = (bf16[768,768]{1,0:T(8,128)(2,1)S(1)}, bf16[768,768]{1,0:T(8,128)(2,1)}, u32[]{:S(2)}) copy-start(bf16[768,768]{1,0:T(8,128)(2,1)} %param.5) | copy-start | bytes 3538948
  35.6 139.8 %all-gather.10.cloned.1.call-start = ((), (), s32[]{:S(2)}) async-start(), calls=%async_computation.4 | async-start | bytes 3538944 | tf_op jit(solution)/shard_map/all_gather | solution.py:67
  120.5 115.1 %all-gather.8.cloned.1.call-start = ((), (), s32[]{:S(2)}) async-start(), calls=%async_computation.3 | async-start | bytes 6488064 | tf_op jit(solution)/shard_map/all_gather | solution.py:92
  129.1 28.5 %collective-permute-start = (bf16[96,128,128]{2,1,0:T(8,128)(2,1)}, bf16[96,128,128]{2,1,0:T(8,128)(2,1)}, u32[]{:S(2)}, u32[]{:S(2)}) collective-permute-start(bf16[96,128,128]{2,1,0:T(8,128)(2,1)} %bitcast.51), channel_id=1, source_target_pairs={{0,1},{1,0},{2,3},{3,2},{4,5},{5,4},{6,7},{7,6},{8,9},{9,8},{10,11... | collective-permute-start | bytes 9437192 | tf_op jit(solution)/shard_map/ppermute | solution.py:22
Sparse Core Ops, SparseCore 0:
  37.7 91.3 all-gather.5
  130.9 44.4 all-gather.9
  182.2 53.3 all-gather.7
where the time goes:
time: 253 us; the launch traced here: 252 us
  waiting for transfers between devices  143 us (57%)
  blocking collectives  37.7 us (15%)
  local copies, waits for them, and re-layouts  27.4 us (11%)
  between operations  13.3 us (5%)
  matrix products  12.2 us (5%)
  other arithmetic  11.5 us (5%)
  starting transfers between devices  6.68 us (3%)
    all_to_all x1, waiting for transfers between devices, body(): lax.all_to_all(send_emb, COL, split_axis=0, concat_axis=0, tiled=True)  68.2 us
    all_gather x1, waiting for transfers between devices, body(): whole_spread = lax.all_gather(spread[:, :per_device], COL, tiled=True)  53.4 us
    all_gather x1, blocking collectives, body(): stats = lax.all_gather(jnp.stack([local_max, local_sum]), 'row')  22.3 us
    all_to_all x1, blocking collectives, body(): lax.all_to_all(wanted, COL, split_axis=0, concat_axis=0, tiled=True)  15.3 us
    all_gather x1, waiting for transfers between devices, body(): all_weights = lax.all_gather(local_weights, 'row')  13.1 us
    dot_general x2, matrix products, propagate_using(): jnp.einsum('gtmk,tgkc->gtmc', all_weights, candidates, preferred_element_...  9.73 us
    all_gather x1, waiting for transfers between devices, gather_columns(): same_core = lax.all_gather(x, 'chip', tiled=True).reshape(-1, BLOCK, width)  8.61 us
    reduce_or x1, other arithmetic, body(): in_mask = jnp.any(shifted[:, :, None] == positions[None, None, :], axis=1)  7.22 us
  transfers between devices with their start and end apart: 5, of which 4 were waited for; matrix products, arithmetic and copies ran while one was open for 11% of the time, Pallas kernels for 0%

commit v1 on v0

--- a/solution.py
+++ b/solution.py
@@ -43,8 +43,6 @@
     embedding_tiles = embeds.reshape(blocks_here, BLOCK, width)
     send_emb = embedding_tiles[requested]
     my_labels = lax.dynamic_slice_in_dim(labels, row_pos * per_device, per_device, 1)
-    lanes = -(-per_device // 128) * 128
-    my_labels = jnp.pad(my_labels, ((0, 0), (0, lanes - per_device)))
     all_labels = gather_columns(my_labels)
     shifted = mask_pos - row_pos * span
     shifted = jnp.where((shifted >= 0) & (shifted < span), shifted, span)

time: 253 us -> 253 us (level)
  local copies, waits for them, and re-layouts: 27.4 us -> 37.4 us
  waiting for transfers between devices: 143 us -> 133 us
    all_gather x1, waiting for transfers between devices: 13.1 us -> 2.76 us  [body(): all_weights = lax.all_gather(local_weights, 'row')]
    ppermute x0 -> x1, local copies, waits for them, and re-layouts: none -> 5.04 us  [gather_columns(): other_core = lax.ppermute(same_core, 'core', [(0, 1), (1, 0)])]
    reshape x0 -> x1, local copies, waits for them, and re-layouts: none -> 5.03 us  [gather_columns(): same_core = lax.all_gather(x, 'chip', tiled=True).reshape(-1, BLOCK, width)]
  transfers between devices with their start and end apart: 5 -> 5, of which waited for: 4 -> 4; matrix products, arithmetic and copies ran while one was open for 11% -> 15% of each run, Pallas kernels for 0% -> 0%
where the time goes in v1:
time: 253 us; the launch traced here: 252 us
  waiting for transfers between devices  133 us (53%)
  blocking collectives  38.2 us (15%)
  local copies, waits for them, and re-layouts  37.4 us (15%)
  between operations  13.3 us (5%)
  matrix products  12.3 us (5%)
  other arithmetic  11.5 us (5%)
  starting transfers between devices  6.68 us (3%)
    all_to_all x1, waiting for transfers between devices, body(): lax.all_to_all(send_emb, COL, split_axis=0, concat_axis=0, tiled=True)  68.3 us
    all_gather x1, waiting for transfers between devices, body(): whole_spread = lax.all_gather(spread[:, :per_device], COL, tiled=True)  53.4 us
    all_gather x1, blocking collectives, body(): stats = lax.all_gather(jnp.stack([local_max, local_sum]), 'row')  22.8 us
    all_to_all x1, blocking collectives, body(): lax.all_to_all(wanted, COL, split_axis=0, concat_axis=0, tiled=True)  15.3 us
    dot_general x2, matrix products, propagate_using(): jnp.einsum('gtmk,tgkc->gtmc', all_weights, candidates, preferred_element_...  9.79 us
    all_gather x1, waiting for transfers between devices, gather_columns(): same_core = lax.all_gather(x, 'chip', tiled=True).reshape(-1, BLOCK, width)  8.61 us
    reduce_or x1, other arithmetic, body(): in_mask = jnp.any(shifted[:, :, None] == positions[None, None, :], axis=1)  7.22 us
    gather x1, local copies, waits for them, and re-layouts, propagate_using(): candidates = gathered[pattern]  5.46 us
  transfers between devices with their start and end apart: 5, of which 4 were waited for; matrix products, arithmetic and copies ran while one was open for 15% of the time, Pallas kernels for 0%

profile of v1, /device:TPU:1, one launch (start us, length us, event | category | flops | bytes accessed | tf_op | source)
XLA Modules:
  0.0 252.4 jit_solution(2643459462821795853)
XLA Ops:
  6.5 0.0 copy-start
  6.5 0.8 fusion.23
  7.4 0.7 compare_select_fusion.1
  8.1 0.1 compare_select_fusion.3
  8.1 0.1 fusion.22
  8.2 0.1 copy.47
  8.3 15.3 %all_to_all.17 = s32[32,1,1]{2,1,0:T(1,128)S(1)} all-to-all(s32[32,1,1]{2,1,0:T(1,128)S(1)} %copy.47), channel_id=1, replica_groups=mesh['row'=8,'chip'=16,'core'=2] {'chip','core'}, dimensions={0} | all-to-all | bytes 256 | tf_op jit(solution)/shard_map/all_to_all | solution.py:42
  23.7 0.7 reduce.1
  24.4 4.9 %gather_fusion = bf16[32,128,768]{2,1,0:T(8,128)(2,1)} fusion(bf16[6,128,768]{2,1,0:T(8,128)(2,1)} %bitcast.52, s32[1024]{0:T(1024)S(1)} %pad_clamp_fusion.3), kind=kCustom, calls=%fused_computation | custom fusion | bytes 12583040 | tf_op jit(solution)/shard_map/gather | solution.py:44
  29.2 0.0 copy-start.3
  29.2 0.0 copy-start.4
  29.2 5.3 %all-to-all-start.1 = ((bf16[32,128,768]{2,1,0:T(8,128)(2,1)}), bf16[32,128,768]{2,1,0:T(8,128)(2,1)}, u32[]{:S(2)}, u32[]{:S(2)}) async-start(bf16[32,128,768]{2,1,0:T(8,128)(2,1)} %gather_fusion), calls=%async_computation.1 | async-start | bytes 12582912 | tf_op jit(solution)/shard_map/all_to_all | solution.py:53
  34.5 0.0 all-gather.6.cloned.1.call-start
  34.6 0.0 copy-done
  34.6 0.1 constant_dynamic-slice_fusion
  34.6 0.0 copy-start.1
  34.6 0.8 copy.58
  35.5 0.0 all-gather.6.cloned.1.call-update
  35.5 0.0 all-gather.10.cloned.1.call-start
  35.5 0.1 reshape.92
  35.6 0.0 copy-done.3
  35.7 7.2 %fusion = pred[768,256]{1,0:T(8,128)(4,1)S(1)} fusion(s32[768,50]{0,1:T(8,128)S(1)} %and_select_fusion), kind=kLoop, calls=%fused_computation.6 | loop fusion | flops 19464192 | bytes 350208 | tf_op jit(solution)/shard_map/reduce_or | solution.py:50
  42.9 0.3 copy.49
  43.2 0.0 copy-done.4
  43.2 68.3 %all-to-all-done.1 = bf16[32,128,768]{2,1,0:T(8,128)(2,1)} async-done(((bf16[32,128,768]{2,1,0:T(8,128)(2,1)}), bf16[32,128,768]{2,1,0:T(8,128)(2,1)}, u32[]{:S(2)}, u32[]{:S(2)}) %all-to-all-start.1) | async-done | bytes 6291488 | tf_op jit(solution)/shard_map/all_to_all | solution.py:53
  111.5 5.2 %gather_fusion.1 = bf16[12,128,768]{2,1,0:T(8,128)(2,1)} fusion(bf16[32,128,768]{2,1,0:T(8,128)(2,1)} %all-to-all-done.1, s32[1024]{0:T(1024)S(1)} %pad_clamp_fusion.2), kind=kCustom, calls=%fused_computation.1 | custom fusion | bytes 4718640 | tf_op jit(solution)/shard_map/gather | solution.py:54
  116.8 0.0 copy-done.1
  116.8 2.5 select_reduce_fusion
  119.3 0.2 fusion.15
  119.5 1.0 copy.50
  120.4 0.0 all-gather.10.cloned.1.call-update
  120.5 0.0 all-gather.8.cloned.1.call-start
  120.5 8.6 %all-gather.6.cloned.1.call-done = bf16[12288,125]{1,0:T(8,128)(2,1)} async-done(((bf16[768,125]{1,0:T(8,128)(2,1)}), bf16[12288,125]{1,0:T(8,128)(2,1)}) %all-gather.6.cloned.1.call-update) | async-done | bytes 3072016 | tf_op jit(solution)/shard_map/all_gather | solution.py:21
  129.1 5.0 %copy.52 = bf16[96,128,125]{1,0,2:T(8,128)(2,1)} copy(bf16[96,128,125]{2,1,0:T(8,128)(2,1)} %bitcast.54) | data formatting | bytes 6144000 | tf_op jit(solution)/shard_map/reshape | solution.py:21
  134.2 1.3 collective-permute-start
  135.4 0.1 reshape.100
  135.5 0.1 broadcast_in_dim.63
  135.6 4.6 %gather_fusion.2 = bf16[96,128,125]{2,1,0:T(8,128)(2,1)} fusion(bf16[96,128,125]{2,1,0:T(8,128)(2,1)} %bitcast.55, s32[1024]{0:T(1024)S(1)} %pad_clamp_fusion.1), kind=kCustom, calls=%fused_computation.2 | custom fusion | bytes 6144384 | tf_op jit(solution)/shard_map/gather | solution.py:80
  140.2 22.8 %all-gather.1 = f32[16,6,128]{2,1,0:T(8,128)S(1)} all-gather(f32[2,6,128]{2,1,0:T(8,128)S(1)} %pad_maximum_fusion), channel_id=3, replica_groups=mesh['row'=8,'chip'=16,'core'=2] {'row'}, dimensions={0}, use_global_device_ids=true | all-gather | bytes 55296 | tf_op jit(solution)/shard_map/all_gather | solution.py:64
  163.1 0.0 collective-permute-done
  163.1 5.0 %copy.53 = bf16[96,128,125]{2,1,0:T(8,128)(2,1)} copy(bf16[96,128,125]{1,0,2:T(8,128)(2,1)} %collective-permute-done) | data formatting | bytes 6144000 | tf_op jit(solution)/shard_map/ppermute | solution.py:22
  168.2 4.6 %gather_fusion.3 = bf16[96,128,125]{2,1,0:T(8,128)(2,1)} fusion(bf16[96,128,125]{2,1,0:T(8,128)(2,1)} %copy.53, s32[1024]{0:T(1024)S(1)} %pad_clamp_fusion.1), kind=kCustom, calls=%fused_computation.3 | custom fusion | bytes 6144384 | tf_op jit(solution)/shard_map/gather | solution.py:80
  172.8 2.8 %all-gather.10.cloned.1.call-done = bf16[48,128,256]{2,1,0:T(8,128)(2,1)} async-done(((bf16[6,128,256]{2,1,0:T(8,128)(2,1)}), bf16[48,128,256]{2,1,0:T(8,128)(2,1)}) %all-gather.10.cloned.1.call-update) | async-done | bytes 3145744 | tf_op jit(solution)/shard_map/all_gather | solution.py:65
  175.6 0.0 copy-start.2
  175.6 5.9 %convert_reduce_fusion.1 = f32[6,128,125]{2,1,0:T(8,128)S(1)} fusion(f32[8,6,128]{2,1,0:T(8,128)S(1)} %fusion.21, bf16[8,6,128,256]{3,2,1,0:T(8,128)(2,1)} %bitcast.68, bf16[6,8,256,125]{3,2,1,0:T(8,128)(2,1)} %bitcast.56, bf16[6,8,256,125]{3,2,1,0:T(8,128)(2,1)} %bitcast.57, pred[6,8,256]{2,1,0:T(8,128)(4,1)S(1)} %broadcast_in_dim.64), kind=kOutput, calls=%fused_computation.13 | convolution fusion | flops 397728000 | bytes 9710592 | tf_op jit(solution)/shard_map/gtmk,tgkc->gtmc/dot_general | solution.py:82
  181.5 0.0 copy-done.2
  181.5 0.7 fusion.17
  182.3 0.0 all-gather.8.cloned.1.call-update
  182.3 0.1 reshape.116
  182.4 53.4 %all-gather.8.cloned.1.call-done = bf16[24576,125]{1,0:T(8,128)(2,1)} async-done(((bf16[768,125]{1,0:T(8,128)(2,1)}), bf16[24576,125]{1,0:T(8,128)(2,1)}) %all-gather.8.cloned.1.call-update) | async-done | bytes 6144016 | tf_op jit(solution)/shard_map/all_gather | solution.py:90
  235.8 5.5 %gather_fusion.4 = bf16[96,128,125]{2,1,0:T(8,128)(2,1)} fusion(bf16[192,128,125]{2,1,0:T(8,128)(2,1)} %bitcast.60, s32[1024]{0:T(1024)S(1)} %pad_clamp_fusion), kind=kCustom, calls=%fused_computation.4 | custom fusion | bytes 6144384 | tf_op jit(solution)/shard_map/gather | solution.py:77
  241.3 3.9 %convert_reduce_fusion = f32[6,128,125]{2,1,0:T(8,128)S(1)} fusion(f32[8,6,128]{2,1,0:T(8,128)S(1)} %fusion.21, bf16[8,6,128,256]{3,2,1,0:T(8,128)(2,1)} %bitcast.69, bf16[6,8,256,125]{3,2,1,0:T(8,128)(2,1)} %bitcast.58), kind=kOutput, calls=%fused_computation.11 | convolution fusion | flops 396192000 | bytes 6626304 | tf_op jit(solution)/shard_map/gtmk,tgkc->gtmc/dot_general | solution.py:82
  245.2 0.7 fusion.16
  (14 shorter events, 0.2 us)
Async XLA Ops:
  6.5 28.0 %copy-start = (bf16[768,1000]{0,1:T(8,128)(2,1)S(1)}, bf16[768,1000]{0,1:T(8,128)(2,1)}, u32[]{:S(2)}) copy-start(bf16[768,1000]{0,1:T(8,128)(2,1)} %param.6) | copy-start | bytes 4608004
  29.2 6.4 %copy-start.3 = (s32[768,50]{0,1:T(8,128)S(1)}, s32[768,50]{0,1:T(8,128)}, u32[]{:S(2)}) copy-start(s32[768,50]{0,1:T(8,128)} %param.9) | copy-start | bytes 460804
  29.2 14.0 %copy-start.4 = (f32[768]{0:T(1024)S(1)}, f32[768]{0:T(1024)}, u32[]{:S(2)}) copy-start(f32[768]{0:T(1024)} %param.7) | copy-start | bytes 9220
  29.2 82.3 %all-to-all-start.1 = ((bf16[32,128,768]{2,1,0:T(8,128)(2,1)}), bf16[32,128,768]{2,1,0:T(8,128)(2,1)}, u32[]{:S(2)}, u32[]{:S(2)}) async-start(bf16[32,128,768]{2,1,0:T(8,128)(2,1)} %gather_fusion), calls=%async_computation.1 | async-start | bytes 12582912 | tf_op jit(solution)/shard_map/all_to_all | solution.py:53
  34.5 94.6 %all-gather.6.cloned.1.call-start = ((), (), s32[]{:S(2)}) async-start(), calls=%async_computation.2 | async-start | bytes 3342336 | tf_op jit(solution)/shard_map/all_gather | solution.py:21
  34.6 82.1 %copy-start.1 = (bf16[768,768]{1,0:T(8,128)(2,1)S(1)}, bf16[768,768]{1,0:T(8,128)(2,1)}, u32[]{:S(2)}) copy-start(bf16[768,768]{1,0:T(8,128)(2,1)} %param.5) | copy-start | bytes 3538948
  35.5 140.1 %all-gather.10.cloned.1.call-start = ((), (), s32[]{:S(2)}) async-start(), calls=%async_computation.4 | async-start | bytes 3538944 | tf_op jit(solution)/shard_map/all_gather | solution.py:65
  120.5 115.3 %all-gather.8.cloned.1.call-start = ((), (), s32[]{:S(2)}) async-start(), calls=%async_computation.3 | async-start | bytes 6488064 | tf_op jit(solution)/shard_map/all_gather | solution.py:90
  134.2 29.0 %collective-permute-start = (bf16[96,128,125]{1,0,2:T(8,128)(2,1)}, bf16[96,128,125]{1,0,2:T(8,128)(2,1)}, u32[]{:S(2)}, u32[]{:S(2)}) collective-permute-start(bf16[96,128,125]{1,0,2:T(8,128)(2,1)} %copy.52), channel_id=1, source_target_pairs={{0,1},{1,0},{2,3},{3,2},{4,5},{5,4},{6,7},{7,6},{8,9},{9,8},{10,11... | collective-permute-start | bytes 9216008 | tf_op jit(solution)/shard_map/ppermute | solution.py:22
  175.6 6.0 %copy-start.2 = (bf16[768,125]{1,0:T(8,128)(2,1)S(1)}, bf16[768,125]{1,0:T(8,128)(2,1)}, u32[]{:S(2)}) copy-start(bf16[768,125]{1,0:T(8,128)(2,1)} %copy.58) | copy-start | bytes 576004
Sparse Core Ops, SparseCore 0:
  37.7 91.3 all-gather.5
  130.9 44.6 all-gather.9
  182.4 53.3 all-gather.7

commit v2 on v0

--- a/solution.py
+++ b/solution.py
@@ -53,7 +53,10 @@
     in_mask = in_mask.reshape(blocks_here, BLOCK, span)
 
     fetched_emb = lax.all_to_all(send_emb, COL, split_axis=0, concat_axis=0, tiled=True)
-    candidate_ids = fetched_emb[my_owners].reshape(blocks_here, span, width)
+    candidate_ids = jnp.stack([
+        lax.dynamic_index_in_dim(fetched_emb, my_owners[t, s], 0, keepdims=False)
+        for t in range(blocks_here) for s in range(slots_here)
+    ]).reshape(blocks_here, span, width)
     scores = jnp.einsum(
         "evg,erg->evr", embedding_tiles, candidate_ids, preferred_element_type=jnp.float32
     ) / math.sqrt(width)

time: 253 us -> 253 us (level)
  waiting for transfers between devices: 143 us -> 112 us
  between operations: 13.3 us -> 36 us
  local copies, waits for them, and re-layouts: 27.4 us -> 34.4 us
  blocking collectives: 37.7 us -> 41 us
    all_to_all x1, waiting for transfers between devices: 68.2 us -> 45 us  [body(): lax.all_to_all(send_emb, COL, split_axis=0, concat_axis=0, tiled=True)]
    unnamed x9 -> x20, local copies, waits for them, and re-layouts: 0.19 us -> 10.6 us
    gather x1 -> x0, local copies, waits for them, and re-layouts: 5.24 us -> none  [body(): candidate_ids = fetched_emb[my_owners].reshape(blocks_here, span, width)]
    all_gather x1, waiting for transfers between devices: 8.61 us -> 4.07 us  [gather_columns(): same_core = lax.all_gather(x, 'chip', tiled=True).reshape(-1, BLOCK, width)]
    all_gather x1, blocking collectives: 22.3 us -> 25.7 us  [body(): stats = lax.all_gather(jnp.stack([local_max, local_sum]), 'row')]
    all_gather x1, waiting for transfers between devices: 13.1 us -> 9.81 us  [body(): all_weights = lax.all_gather(local_weights, 'row')]
  transfers between devices with their start and end apart: 5 -> 5, of which waited for: 4 -> 4; matrix products, arithmetic and copies ran while one was open for 11% -> 13% of each run, Pallas kernels for 0% -> 0%
where the time goes in v2:
time: 253 us; the launch traced here: 252 us
  waiting for transfers between devices  112 us (44%)
  blocking collectives  41 us (16%)
  between operations  36 us (14%)
  local copies, waits for them, and re-layouts  34.4 us (14%)
  other arithmetic  11.4 us (5%)
  matrix products  10.5 us (4%)
  starting transfers between devices  6.7 us (3%)
    all_gather x1, waiting for transfers between devices, body(): whole_spread = lax.all_gather(spread[:, :per_device], COL, tiled=True)  53.3 us
    all_to_all x1, waiting for transfers between devices, body(): lax.all_to_all(send_emb, COL, split_axis=0, concat_axis=0, tiled=True)  45 us
    all_gather x1, blocking collectives, body(): stats = lax.all_gather(jnp.stack([local_max, local_sum]), 'row')  25.7 us
    all_to_all x1, blocking collectives, body(): lax.all_to_all(wanted, COL, split_axis=0, concat_axis=0, tiled=True)  15.3 us
    unnamed x20, local copies, waits for them, and re-layouts  10.6 us
    all_gather x1, waiting for transfers between devices, body(): all_weights = lax.all_gather(local_weights, 'row')  9.81 us
    dot_general x2, matrix products, propagate_using(): jnp.einsum('gtmk,tgkc->gtmc', all_weights, candidates, preferred_element_...  9.72 us
    reduce_or x1, other arithmetic, body(): in_mask = jnp.any(shifted[:, :, None] == positions[None, None, :], axis=1)  7.22 us
  transfers between devices with their start and end apart: 5, of which 4 were waited for; matrix products, arithmetic and copies ran while one was open for 13% of the time, Pallas kernels for 0%

profile of v2, /device:TPU:1, one launch (start us, length us, event | category | flops | bytes accessed | tf_op | source)
XLA Modules:
  0.0 252.2 jit_solution(13979857251894267688)
XLA Ops:
  6.5 0.0 copy-start
  6.5 0.8 fusion.23
  7.4 0.7 compare_select_fusion.1
  8.1 0.1 constant_dynamic-slice_fusion.1
  8.1 0.1 fusion.22
  8.2 0.1 copy.42
  8.3 15.3 %all_to_all.17 = s32[32,1,1]{2,1,0:T(1,128)S(1)} all-to-all(s32[32,1,1]{2,1,0:T(1,128)S(1)} %copy.42), channel_id=1, replica_groups=mesh['row'=8,'chip'=16,'core'=2] {'chip','core'}, dimensions={0} | all-to-all | bytes 256 | tf_op jit(solution)/shard_map/all_to_all | solution.py:42
  23.7 0.7 reduce.1
  24.4 4.9 %gather_fusion = bf16[32,128,768]{2,1,0:T(8,128)(2,1)} fusion(bf16[6,128,768]{2,1,0:T(8,128)(2,1)} %bitcast.61, s32[1024]{0:T(1024)S(1)} %pad_clamp_fusion.2), kind=kCustom, calls=%fused_computation | custom fusion | bytes 12583040 | tf_op jit(solution)/shard_map/gather | solution.py:44
  29.3 0.0 copy-start.2
  29.3 0.0 copy-start.3
  29.3 5.3 %all-to-all-start.1 = ((bf16[32,128,768]{2,1,0:T(8,128)(2,1)}), bf16[32,128,768]{2,1,0:T(8,128)(2,1)}, u32[]{:S(2)}, u32[]{:S(2)}) async-start(bf16[32,128,768]{2,1,0:T(8,128)(2,1)} %gather_fusion), calls=%async_computation.1 | async-start | bytes 12582912 | tf_op jit(solution)/shard_map/all_to_all | solution.py:55
  34.6 0.0 all-gather.6.cloned.1.call-start
  34.6 0.0 copy-done
  34.6 0.1 constant_dynamic-slice_fusion
  34.7 0.2 copy.51
  34.9 0.7 pad.4
  35.6 0.0 copy-start.1
  35.6 0.0 all-gather.6.cloned.1.call-update
  35.6 0.0 all-gather.10.cloned.1.call-start
  35.7 0.7 fusion.30
  51.5 0.0 copy-done.2
  51.5 7.2 %fusion = pred[768,256]{1,0:T(8,128)(4,1)S(1)} fusion(s32[768,50]{0,1:T(8,128)S(1)} %and_select_fusion), kind=kLoop, calls=%fused_computation.5 | loop fusion | flops 19464192 | bytes 350208 | tf_op jit(solution)/shard_map/reduce_or | solution.py:52
  58.7 0.3 copy.44
  66.6 0.0 copy-done.3
  66.6 45.0 %all-to-all-done.1 = bf16[32,128,768]{2,1,0:T(8,128)(2,1)} async-done(((bf16[32,128,768]{2,1,0:T(8,128)(2,1)}), bf16[32,128,768]{2,1,0:T(8,128)(2,1)}, u32[]{:S(2)}, u32[]{:S(2)}) %all-to-all-start.1) | async-done | bytes 6291488 | tf_op jit(solution)/shard_map/all_to_all | solution.py:55
  111.6 0.9 dynamic-slice_dynamic-update-slice_fusion.11
  112.5 0.9 dynamic-slice_dynamic-update-slice_fusion.10
  113.5 0.9 dynamic-slice_dynamic-update-slice_fusion.9
  114.4 0.9 dynamic-slice_dynamic-update-slice_fusion.8
  115.4 0.9 dynamic-slice_dynamic-update-slice_fusion.7
  116.3 0.9 dynamic-slice_dynamic-update-slice_fusion.6
  117.3 1.0 dynamic-slice_dynamic-update-slice_fusion.5
  118.2 1.0 dynamic-slice_dynamic-update-slice_fusion.4
  119.2 0.9 dynamic-slice_dynamic-update-slice_fusion.3
  120.1 0.9 dynamic-slice_dynamic-update-slice_fusion.2
  121.1 0.9 dynamic-slice_dynamic-update-slice_fusion.1
  122.0 0.9 dynamic-slice_dynamic-update-slice_fusion
  123.0 0.0 copy-done.1
  123.0 0.8 select_reduce_fusion
  123.8 0.2 fusion.15
  124.0 1.0 copy.45
  125.0 0.0 all-gather.10.cloned.1.call-update
  125.0 0.0 all-gather.8.cloned.1.call-start
  125.1 4.1 %all-gather.6.cloned.1.call-done = bf16[12288,128]{1,0:T(8,128)(2,1)} async-done(((bf16[768,128]{1,0:T(8,128)(2,1)}), bf16[12288,128]{1,0:T(8,128)(2,1)}) %all-gather.6.cloned.1.call-update) | async-done | bytes 3145744 | tf_op jit(solution)/shard_map/all_gather | solution.py:21
  129.1 1.3 collective-permute-start
  130.4 0.1 reshape.92
  130.5 0.1 broadcast_in_dim.59
  130.6 4.7 %gather_fusion.1 = bf16[96,128,128]{2,1,0:T(8,128)(2,1)} fusion(bf16[96,128,128]{2,1,0:T(8,128)(2,1)} %bitcast.64, s32[1024]{0:T(1024)S(1)} %pad_clamp_fusion.1), kind=kCustom, calls=%fused_computation.1 | custom fusion | bytes 6291840 | tf_op jit(solution)/shard_map/gather | solution.py:85
  135.3 25.7 %all-gather.1 = f32[16,6,128]{2,1,0:T(8,128)S(1)} all-gather(f32[2,6,128]{2,1,0:T(8,128)S(1)} %pad_maximum_fusion), channel_id=3, replica_groups=mesh['row'=8,'chip'=16,'core'=2] {'row'}, dimensions={0}, use_global_device_ids=true | all-gather | bytes 55296 | tf_op jit(solution)/shard_map/all_gather | solution.py:69
  161.0 0.0 collective-permute-done
  161.0 4.6 %gather_fusion.2 = bf16[96,128,128]{2,1,0:T(8,128)(2,1)} fusion(bf16[96,128,128]{2,1,0:T(8,128)(2,1)} %collective-permute-done, s32[1024]{0:T(1024)S(1)} %pad_clamp_fusion.1), kind=kCustom, calls=%fused_computation.2 | custom fusion | bytes 6291840 | tf_op jit(solution)/shard_map/gather | solution.py:85
  165.7 9.8 %all-gather.10.cloned.1.call-done = bf16[48,128,256]{2,1,0:T(8,128)(2,1)} async-done(((bf16[6,128,256]{2,1,0:T(8,128)(2,1)}), bf16[48,128,256]{2,1,0:T(8,128)(2,1)}) %all-gather.10.cloned.1.call-update) | async-done | bytes 3145744 | tf_op jit(solution)/shard_map/all_gather | solution.py:70
  175.5 5.9 %convert_reduce_fusion.1 = f32[6,128,128]{2,1,0:T(8,128)S(1)} fusion(f32[8,6,128]{2,1,0:T(8,128)S(1)} %fusion.21, bf16[8,6,128,256]{3,2,1,0:T(8,128)(2,1)} %bitcast.78, bf16[6,8,256,128]{3,2,1,0:T(8,128)(2,1)} %bitcast.65, bf16[6,8,256,128]{3,2,1,0:T(8,128)(2,1)} %bitcast.66, pred[6,8,256]{2,1,0:T(8,128)(4,1)S(1)} %broadcast_in_dim.60), kind=kOutput, calls=%fused_computation.12 | convolution fusion | flops 407273472 | bytes 9867264 | tf_op jit(solution)/shard_map/gtmk,tgkc->gtmc/dot_general | solution.py:87
  181.4 0.7 fusion.16
  182.1 0.0 all-gather.8.cloned.1.call-update
  182.2 0.1 reshape.108
  182.3 53.3 %all-gather.8.cloned.1.call-done = bf16[24576,125]{1,0:T(8,128)(2,1)} async-done(((bf16[768,125]{1,0:T(8,128)(2,1)}), bf16[24576,125]{1,0:T(8,128)(2,1)}) %all-gather.8.cloned.1.call-update) | async-done | bytes 6144016 | tf_op jit(solution)/shard_map/all_gather | solution.py:95
  235.5 5.5 %gather_fusion.3 = bf16[96,128,125]{2,1,0:T(8,128)(2,1)} fusion(bf16[192,128,125]{2,1,0:T(8,128)(2,1)} %bitcast.69, s32[1024]{0:T(1024)S(1)} %pad_clamp_fusion), kind=kCustom, calls=%fused_computation.3 | custom fusion | bytes 6144384 | tf_op jit(solution)/shard_map/gather | solution.py:82
  241.1 3.9 %convert_reduce_fusion = f32[6,128,125]{2,1,0:T(8,128)S(1)} fusion(f32[8,6,128]{2,1,0:T(8,128)S(1)} %fusion.21, bf16[8,6,128,256]{3,2,1,0:T(8,128)(2,1)} %bitcast.79, bf16[6,8,256,125]{3,2,1,0:T(8,128)(2,1)} %bitcast.67), kind=kOutput, calls=%fused_computation.10 | convolution fusion | flops 396192000 | bytes 6626304 | tf_op jit(solution)/shard_map/gtmk,tgkc->gtmc/dot_general | solution.py:87
  245.0 0.7 fusion.17
  (13 shorter events, 0.2 us)
Async XLA Ops:
  6.5 28.1 %copy-start = (bf16[768,1000]{0,1:T(8,128)(2,1)S(1)}, bf16[768,1000]{0,1:T(8,128)(2,1)}, u32[]{:S(2)}) copy-start(bf16[768,1000]{0,1:T(8,128)(2,1)} %param.6) | copy-start | bytes 4608004
  29.3 22.2 %copy-start.2 = (s32[768,50]{0,1:T(8,128)S(1)}, s32[768,50]{0,1:T(8,128)}, u32[]{:S(2)}) copy-start(s32[768,50]{0,1:T(8,128)} %param.9) | copy-start | bytes 460804
  29.3 37.3 %copy-start.3 = (f32[768]{0:T(1024)S(1)}, f32[768]{0:T(1024)}, u32[]{:S(2)}) copy-start(f32[768]{0:T(1024)} %param.7) | copy-start | bytes 9220
  29.3 82.3 %all-to-all-start.1 = ((bf16[32,128,768]{2,1,0:T(8,128)(2,1)}), bf16[32,128,768]{2,1,0:T(8,128)(2,1)}, u32[]{:S(2)}, u32[]{:S(2)}) async-start(bf16[32,128,768]{2,1,0:T(8,128)(2,1)} %gather_fusion), calls=%async_computation.1 | async-start | bytes 12582912 | tf_op jit(solution)/shard_map/all_to_all | solution.py:55
  34.6 94.6 %all-gather.6.cloned.1.call-start = ((), (), s32[]{:S(2)}) async-start(), calls=%async_computation.2 | async-start | bytes 3342336 | tf_op jit(solution)/shard_map/all_gather | solution.py:21
  35.6 87.4 %copy-start.1 = (bf16[768,768]{1,0:T(8,128)(2,1)S(1)}, bf16[768,768]{1,0:T(8,128)(2,1)}, u32[]{:S(2)}) copy-start(bf16[768,768]{1,0:T(8,128)(2,1)} %param.5) | copy-start | bytes 3538948
  35.6 139.9 %all-gather.10.cloned.1.call-start = ((), (), s32[]{:S(2)}) async-start(), calls=%async_computation.4 | async-start | bytes 3538944 | tf_op jit(solution)/shard_map/all_gather | solution.py:70
  125.0 110.5 %all-gather.8.cloned.1.call-start = ((), (), s32[]{:S(2)}) async-start(), calls=%async_computation.3 | async-start | bytes 6488064 | tf_op jit(solution)/shard_map/all_gather | solution.py:95
  129.1 31.9 %collective-permute-start = (bf16[96,128,128]{2,1,0:T(8,128)(2,1)}, bf16[96,128,128]{2,1,0:T(8,128)(2,1)}, u32[]{:S(2)}, u32[]{:S(2)}) collective-permute-start(bf16[96,128,128]{2,1,0:T(8,128)(2,1)} %bitcast.63), channel_id=1, source_target_pairs={{0,1},{1,0},{2,3},{3,2},{4,5},{5,4},{6,7},{7,6},{8,9},{9,8},{10,11... | collective-permute-start | bytes 9437192 | tf_op jit(solution)/shard_map/ppermute | solution.py:22
Sparse Core Ops, SparseCore 0:
  37.8 91.2 all-gather.5
  130.9 44.5 all-gather.9
  182.3 53.2 all-gather.7
